TPU v7x, 32 devices: a whole 2x2x4 slice. The times are simulated.
32 devices in a mesh: grp: 2 (over y), ctx: 2 (over core), tp: 8 (over z, x).
Axes of the slice: x: 2, y: 2, z: 4, core: 2. Of those that a mesh axis runs over, the one named last changes fastest.
Arguments:
- queries: bfloat16 [8192, 8, 192], P(('grp', 'ctx'), 'tp'), parts along dimension 0, may hold values from -70 to 70
- latent_rows: bfloat16 [8192, 576], P(('grp', 'ctx', 'tp')), parts along dimension 0, may hold values from -6 to 6
- doc_ids: int32 [8192], P(('grp', 'ctx', 'tp')), parts along dimension 0, may hold values from 0 to 7, as said below
- key_weight: bfloat16 [512, 1024], P(None, 'tp'), may hold values from -0.25 to 0.25
- value_weight: bfloat16 [512, 1024], P(None, 'tp'), may hold values from -0.25 to 0.25
Outputs:
- attended: bfloat16 [8192, 1024], P(('grp', 'ctx'), 'tp'), parts along dimension 0
There are 2 independent parts, one for each index of `grp`. A program takes and returns all parts, laid end to end along the dimension named above; an argument that names none is the same for every part. Nothing has to cross between parts.
Inputs may be any that keep to these rules, and one draw needn't show every extreme that they name: `doc_ids`: never falling along the tokens.
All inputs are finite; a program needn't handle non-finite values.
Results may differ from a plain program's by a relative error of at most 0.0065.
Values may be sent and summed in bfloat16 or wider, within the bound.
No kernel may reach another device: no remote copies, remote signals or barrier semaphores. Data moves between devices by JAX's collectives and lax.ppermute only.
A program may use at most 64 MiB of HBM per device.

v0:
```python
import functools
import math

import jax
import jax.numpy as jnp
import numpy as np
from jax import lax
from jax.experimental import pallas as pl
from jax.experimental.pallas import tpu as pltpu
from jax.sharding import PartitionSpec as P

KV_RANK = 512
ROPE_DIM = 64
NOPE_DIM = 128
LANES = 128
BLOCK_Q = 512
BLOCK_K = 512
FAR = 1 << 30


def flash_kernel(
    qbase_ref, qdf_ref, qdl_ref, kminp_ref, kmaxp_ref, kmind_ref, kmaxd_ref,
    q_ref, *rest, sets, tiles, factor,
):
    set_refs = [rest[5 * n : 5 * n + 5] for n in range(sets)]
    qd_ref, o_ref = rest[5 * sets], rest[5 * sets + 1]
    qt = pl.program_id(1)
    bq = q_ref.shape[0]
    bk = BLOCK_K
    first_pos = qbase_ref[0] + qt * bq
    last_pos = first_pos + (bq - 1)
    first_doc = qdf_ref[qt]
    last_doc = qdl_ref[qt]
    q = q_ref[...]
    q_nope = q[:, :NOPE_DIM]
    q_rope = q[:, NOPE_DIM:]
    q_pos = first_pos + lax.broadcasted_iota(jnp.int32, (bq, 1), 0)
    q_doc = qd_ref[...]
    nt = (((1,), (1,)), ((), ()))

    m_sc, l_sc, acc_sc = rest[5 * sets + 2 :]
    m_sc[...] = jnp.full(m_sc.shape, -1e30, jnp.float32)
    l_sc[...] = jnp.zeros(l_sc.shape, jnp.float32)
    acc_sc[...] = jnp.zeros(acc_sc.shape, jnp.float32)

    def make_step(number, k_ref, v_ref, r_ref, kp_ref, kd_ref):
        def tile(masked, t):
            start = pl.multiple_of(t * bk, bk)
            keys = k_ref[pl.ds(start, bk), :]
            ropes = r_ref[pl.ds(start, bk), :]
            scores = lax.dot_general(q_nope, keys, nt, preferred_element_type=jnp.float32)
            scores = scores + lax.dot_general(
                q_rope, ropes[:, :ROPE_DIM], nt, preferred_element_type=jnp.float32
            )
            scores = scores * factor
            if masked:
                k_pos = kp_ref[:, pl.ds(start, bk)]
                k_doc = kd_ref[:, pl.ds(start, bk)]
                visible = (k_pos <= q_pos) & (k_doc == q_doc)
                scores = jnp.where(visible, scores, jnp.float32(-1e30))
            m_prev = m_sc[...]
            m_new = jnp.maximum(m_prev, jnp.max(scores, axis=1, keepdims=True))
            alpha = jnp.exp(m_prev - m_new)
            weights = jnp.exp(scores - m_new)
            if masked:
                weights = jnp.where(visible, weights, jnp.float32(0.0))
            l_sc[...] = alpha * l_sc[...] + jnp.sum(weights, axis=1, keepdims=True)
            acc_sc[...] = alpha * acc_sc[...] + jnp.dot(
                weights.astype(jnp.bfloat16),
                v_ref[pl.ds(start, bk), :],
                preferred_element_type=jnp.float32,
            )
            m_sc[...] = m_new

        def step(t, carry):
            at = number * tiles + t
            active = (
                (kminp_ref[at] <= last_pos)
                & (kmaxd_ref[at] >= first_doc)
                & (kmind_ref[at] <= last_doc)
            )
            full = (
                (kmaxp_ref[at] <= first_pos)
                & (kmind_ref[at] == last_doc)
                & (kmaxd_ref[at] == first_doc)
            )

            @pl.when(active & full)
            def _():
                tile(False, t)

            @pl.when(active & jnp.logical_not(full))
            def _():
                tile(True, t)

            return carry

        return step

    for number, refs in enumerate(set_refs):
        lax.fori_loop(0, tiles, make_step(number, *refs), 0)
    o_ref[...] = (acc_sc[...] / l_sc[...]).astype(o_ref.dtype)


def flash(query_heads, packs, positions, pos_tables, docs_rows, query_docs, query_base):
    heads_here, rows, _ = query_heads.shape
    count = packs[0].shape[0]
    bq = min(BLOCK_Q, rows)
    bk = BLOCK_K
    q_tiles = rows // bq
    tiles = count // bk
    sets = len(packs)
    qdf = query_docs[::bq]
    qdl = query_docs[bq - 1 :: bq]
    kminp, kmaxp = pos_tables
    doc_tiles = jnp.concatenate(docs_rows, axis=0).reshape(sets * tiles, bk)
    kmind = jnp.min(doc_tiles, axis=1)
    kmaxd = jnp.max(doc_tiles, axis=1)

    in_specs = [pl.BlockSpec((None, bq, query_heads.shape[2]), lambda h, qt, *_: (h, qt, 0))]
    operands = [query_heads]
    for pack, pos, doc in zip(packs, positions, docs_rows):
        in_specs += [
            pl.BlockSpec((count, LANES), lambda h, qt, *_: (0, h)),
            pl.BlockSpec((count, LANES), lambda h, qt, *_: (0, heads_here + h)),
            pl.BlockSpec((count, LANES), lambda h, qt, *_: (0, 2 * heads_here)),
            pl.BlockSpec((1, count), lambda h, qt, *_: (0, 0)),
            pl.BlockSpec((1, count), lambda h, qt, *_: (0, 0)),
        ]
        operands += [pack, pack, pack, pos, doc.reshape(1, count)]
    in_specs.append(pl.BlockSpec((bq, 1), lambda h, qt, *_: (qt, 0)))
    operands.append(query_docs.reshape(rows, 1))

    kernel = functools.partial(
        flash_kernel, sets=sets, tiles=tiles, factor=1.0 / math.sqrt(NOPE_DIM + ROPE_DIM)
    )
    grid_spec = pltpu.PrefetchScalarGridSpec(
        num_scalar_prefetch=7,
        grid=(heads_here, q_tiles),
        in_specs=in_specs,
        out_specs=pl.BlockSpec((bq, LANES), lambda h, qt, *_: (qt, h)),
        scratch_shapes=[
            pltpu.VMEM((bq, 1), jnp.float32),
            pltpu.VMEM((bq, 1), jnp.float32),
            pltpu.VMEM((bq, LANES), jnp.float32),
        ],
    )
    return pl.pallas_call(
        kernel,
        grid_spec=grid_spec,
        out_shape=jax.ShapeDtypeStruct((rows, heads_here * LANES), jnp.bfloat16),
        compiler_params=pltpu.CompilerParams(dimension_semantics=("arbitrary", "arbitrary")),
    )(query_base, qdf, qdl, kminp, kmaxp, kmind, kmaxd, *operands)


def ring_tables(order):
    count = len(order)
    place = {device: number for number, device in enumerate(order)}
    ahead = count // 2
    behind = count - 1 - ahead
    sources = [list(range(count))]
    for step in range(1, ahead + 1):
        sources.append([order[(place[d] - step) % count] for d in range(count)])
        if step <= behind:
            sources.append([order[(place[d] + step) % count] for d in range(count)])
    source_of = np.zeros((count, count), np.int32)
    slot_of = np.zeros((count, count), np.int32)
    for number, row in enumerate(sources):
        for device, source in enumerate(row):
            source_of[device, number] = source
            slot_of[device, source] = number
    me = lax.axis_index("tp")
    return jnp.asarray(source_of)[me], jnp.asarray(slot_of)[me]


def ring_gather(block, order, early):
    count = len(order)
    place = {device: number for number, device in enumerate(order)}
    forward = [(order[i], order[(i + 1) % count]) for i in range(count)]
    backward = [(order[(i + 1) % count], order[i]) for i in range(count)]
    ahead = count // 2
    behind = count - 1 - ahead
    arrived = [block]
    moving_f = block
    moving_b = block
    for step in range(1, ahead + 1):
        moving_f = lax.ppermute(moving_f, "tp", forward)
        if step <= behind:
            moving_b = lax.ppermute(moving_b, "tp", backward)
        if step == 1:
            moving_f, moving_b, early = lax.optimization_barrier((moving_f, moving_b, early))
        arrived.append(moving_f)
        if step <= behind:
            arrived.append(moving_b)
    return jnp.concatenate(arrived, axis=0), early


def body(queries, latent_rows, doc_ids, key_weight, value_weight, *, order):
    block_rows = queries.shape[0]
    chunk_rows = latent_rows.shape[0]
    chunks = block_rows // chunk_rows
    cycle_size = lax.axis_size("ctx")
    cycle_index = lax.axis_index("ctx")
    heads_here = key_weight.shape[1] // NOPE_DIM
    width = latent_rows.shape[1]
    pad = (-(width + 1)) % LANES
    doc_column = jnp.concatenate(
        [doc_ids.astype(jnp.bfloat16)[:, None], jnp.zeros((chunk_rows, pad), jnp.bfloat16)],
        axis=1,
    )
    chunk = jnp.concatenate([latent_rows, doc_column], axis=1)
    source_of, slot_of = ring_tables(order)
    offsets = (
        source_of[:, None] * chunk_rows + jnp.arange(chunk_rows, dtype=jnp.int32)[None, :]
    ).reshape(block_rows)
    positions = []
    for distance in range(cycle_size - 1, 0, -1):
        source = cycle_index - distance
        positions.append(jnp.where(source >= 0, source * block_rows + offsets, FAR))
    positions.append(cycle_index * block_rows + offsets)
    pos_tiles = jnp.concatenate(positions, axis=0).reshape(-1, BLOCK_K)
    pos_tables = (jnp.min(pos_tiles, axis=1), jnp.max(pos_tiles, axis=1))
    query_base = (cycle_index * block_rows).astype(jnp.int32).reshape(1)
    query_heads = jnp.transpose(queries, (1, 0, 2))
    early = (tuple(pos.reshape(1, -1) for pos in positions), pos_tables, query_base, query_heads)
    gathered, early = ring_gather(chunk, order, early)
    positions, pos_tables, query_base, query_heads = early
    latent_part = gathered[:, :KV_RANK]
    key_heads = jnp.dot(latent_part, key_weight, preferred_element_type=jnp.float32).astype(
        jnp.bfloat16
    )
    value_heads = jnp.dot(latent_part, value_weight, preferred_element_type=jnp.float32).astype(
        jnp.bfloat16
    )
    pack = jnp.concatenate([key_heads, value_heads, gathered[:, KV_RANK:]], axis=1)
    docs = gathered[:, width].astype(jnp.int32)
    query_docs = jnp.take(docs.reshape(chunks, chunk_rows), slot_of, axis=0).reshape(block_rows)

    packs, docs_rows = [], []
    for distance in range(cycle_size - 1, 0, -1):
        route = [(i - distance, i) for i in range(cycle_size) if i - distance >= 0]
        moved = lax.ppermute(pack, "ctx", route)
        packs.append(moved)
        docs_rows.append(moved[:, 2 * heads_here * NOPE_DIM + ROPE_DIM].astype(jnp.int32))
    packs.append(pack)
    docs_rows.append(docs)
    return flash(query_heads, packs, positions, pos_tables, docs_rows, query_docs, query_base)


def ring_order(mesh):
    line = list(mesh.devices[(0,) * (mesh.devices.ndim - 1)].reshape(-1))
    try:
        where = {(d.coords[0], d.coords[2]): number for number, d in enumerate(line)}
        xs = sorted({key[0] for key in where})
        zs = sorted({key[1] for key in where})
        order = []
        for turn, x in enumerate(xs):
            for z in zs if turn % 2 == 0 else zs[::-1]:
                order.append(where[(x, z)])
    except (AttributeError, KeyError, IndexError, TypeError):
        return list(range(len(line)))
    if sorted(order) != list(range(len(line))):
        return list(range(len(line)))
    return order


def solution(mesh):
    placed = (
        P(("grp", "ctx"), "tp", None),
        P(("grp", "ctx", "tp"), None),
        P(("grp", "ctx", "tp")),
        P(None, "tp"),
        P(None, "tp"),
    )
    return jax.shard_map(
        functools.partial(body, order=ring_order(mesh)),
        mesh=mesh,
        in_specs=placed,
        out_specs=P(("grp", "ctx"), "tp"),
        check_vma=False,
    )
```

profile of v0, /device:TPU:17, one launch (start us, length us, event | category | flops | bytes accessed | tf_op | source)
XLA Modules:
  0.0 77.7 jit_solution(16679823996506274298)
XLA Ops:
  0.0 0.0 copy-start
  0.0 1.2 %copy.18 = bf16[256,576]{1,0:T(8,128)(2,1)S(1)} copy(bf16[256,576]{0,1:T(8,128)(2,1)} %param.8) | data formatting | bytes 589824 | tf_op args[1]
  1.2 0.7 convert_element_type.49
  1.9 0.1 broadcast_in_dim.29
  2.0 0.1 pad.12.clone
  2.1 0.8 %constant_dynamic-update-slice_fusion.7 = (bf16[2048,640]{1,0:T(8,128)(2,1)S(1)}, bf16[256,640]{1,0:T(8,128)(2,1)}) fusion(bf16[640]{0:T(1024)(128)(2,1)S(1)} %pad.12.clone, bf16[256,1]{1,0:T(8,128)(2,1)S(1)} %broadcast_in_dim.29, bf16[256,576]{1,0:T(8,128)(2,1)S(1)} %copy.18), kind=kLoop, calls=%fused_computation.21 | loop fusion | flops 983039 | bytes 952064
  2.9 1.3 %collective-permute-start = (bf16[256,640]{1,0:T(8,128)(2,1)}, bf16[256,640]{1,0:T(8,128)(2,1)S(1)}, u32[]{:S(2)}, u32[]{:S(2)}) collective-permute-start(bf16[256,640]{1,0:T(8,128)(2,1)} %get-tuple-element.26), channel_id=1, source_target_pairs={{0,2},{2,4},{4,6},{6,7},{7,5},{5,3},{3,1},{1,0},{8,10},{10,12},{12... | collective-permute-start | bytes 983048 | tf_op jit(solution)/shard_map/ppermute | solution.py:187
  4.2 0.2 collective-permute-start.1
  4.4 0.7 fusion.5
  5.1 0.1 mul.26
  5.2 0.1 broadcast_bitcast_fusion
  5.2 0.1 add_bitcast_fusion
  5.3 0.6 copy.26
  5.9 0.6 copy.27
  6.5 2.2 %copy.20 = bf16[2048,1,192]{2,0,1:T(8,128)(2,1)} copy(bf16[2048,1,192]{0,2,1:T(8,128)(2,1)} %param.7) | data formatting | bytes 1572864 | tf_op args[0]
  8.8 0.7 fusion.2
  9.5 2.2 %collective-permute-done = bf16[256,640]{1,0:T(8,128)(2,1)S(1)} collective-permute-done((bf16[256,640]{1,0:T(8,128)(2,1)}, bf16[256,640]{1,0:T(8,128)(2,1)S(1)}, u32[]{:S(2)}, u32[]{:S(2)}) %collective-permute-start) | collective-permute-done | bytes 327712 | tf_op jit(solution)/shard_map/ppermute | solution.py:187
  11.7 1.0 %collective-permute-done.1 = bf16[256,640]{1,0:T(8,128)(2,1)S(1)} collective-permute-done((bf16[256,640]{1,0:T(8,128)(2,1)}, bf16[256,640]{1,0:T(8,128)(2,1)S(1)}, u32[]{:S(2)}, u32[]{:S(2)}) %collective-permute-start.1) | collective-permute-done | bytes 327712 | tf_op jit(solution)/shard_map/ppermute | solution.py:189
  12.7 1.2 %collective-permute-start.2 = (bf16[256,640]{1,0:T(8,128)(2,1)S(1)}, bf16[256,640]{1,0:T(8,128)(2,1)S(1)}, u32[]{:S(2)}, u32[]{:S(2)}) collective-permute-start(bf16[256,640]{1,0:T(8,128)(2,1)S(1)} %collective-permute-done), channel_id=1, source_target_pairs={{0,2},{2,4},{4,6},{6,7},{7,5},{5,3},{3,1},{1,0},{8,10},{10,12},{12... | collective-permute-start | bytes 983048 | tf_op jit(solution)/shard_map/ppermute | solution.py:187
  13.9 0.3 collective-permute-start.3
  14.1 5.9 %collective-permute-done.2 = bf16[256,640]{1,0:T(8,128)(2,1)S(1)} collective-permute-done((bf16[256,640]{1,0:T(8,128)(2,1)S(1)}, bf16[256,640]{1,0:T(8,128)(2,1)S(1)}, u32[]{:S(2)}, u32[]{:S(2)}) %collective-permute-start.2) | collective-permute-done | bytes 327712 | tf_op jit(solution)/shard_map/ppermute | solution.py:187
  20.0 1.2 %collective-permute-start.4 = (bf16[256,640]{1,0:T(8,128)(2,1)S(1)}, bf16[256,640]{1,0:T(8,128)(2,1)S(1)}, u32[]{:S(2)}, u32[]{:S(2)}) collective-permute-start(bf16[256,640]{1,0:T(8,128)(2,1)S(1)} %collective-permute-done.2), channel_id=1, source_target_pairs={{0,2},{2,4},{4,6},{6,7},{7,5},{5,3},{3,1},{1,0},{8,10},{10,12},{12... | collective-permute-start | bytes 983048 | tf_op jit(solution)/shard_map/ppermute | solution.py:187
  21.3 0.0 collective-permute-done.3
  21.3 0.3 collective-permute-start.5
  21.7 4.8 %collective-permute-done.4 = bf16[256,640]{1,0:T(8,128)(2,1)S(1)} collective-permute-done((bf16[256,640]{1,0:T(8,128)(2,1)S(1)}, bf16[256,640]{1,0:T(8,128)(2,1)S(1)}, u32[]{:S(2)}, u32[]{:S(2)}) %collective-permute-start.4) | collective-permute-done | bytes 327712 | tf_op jit(solution)/shard_map/ppermute | solution.py:187
  26.4 1.2 %collective-permute-start.6 = (bf16[256,640]{1,0:T(8,128)(2,1)S(1)}, bf16[256,640]{1,0:T(8,128)(2,1)S(1)}, u32[]{:S(2)}, u32[]{:S(2)}) collective-permute-start(bf16[256,640]{1,0:T(8,128)(2,1)S(1)} %collective-permute-done.4), channel_id=1, source_target_pairs={{0,2},{2,4},{4,6},{6,7},{7,5},{5,3},{3,1},{1,0},{8,10},{10,12},{12... | collective-permute-start | bytes 983048 | tf_op jit(solution)/shard_map/ppermute | solution.py:187
  27.7 0.0 collective-permute-done.5
  27.8 0.0 copy-start.5
  27.8 5.2 %collective-permute-done.6 = bf16[256,640]{1,0:T(8,128)(2,1)S(1)} collective-permute-done((bf16[256,640]{1,0:T(8,128)(2,1)S(1)}, bf16[256,640]{1,0:T(8,128)(2,1)S(1)}, u32[]{:S(2)}, u32[]{:S(2)}) %collective-permute-start.6) | collective-permute-done | bytes 327712 | tf_op jit(solution)/shard_map/ppermute | solution.py:187
  33.0 0.0 copy-start.3
  33.1 0.0 copy-done
  33.1 0.7 convolution_convert_fusion
  33.8 0.7 copy-done.3
  34.5 0.0 copy-done.5
  34.5 0.7 convolution_convert_fusion.1
  35.2 0.2 pad_maximum_fusion.rest_5_.rest_6_.rest_7_
  35.4 0.0 copy-start.1
  35.4 1.3 %collective-permute-start.7 = (bf16[2048,384]{1,0:T(8,128)(2,1)S(1)}, bf16[2048,384]{1,0:T(8,128)(2,1)S(1)}, u32[]{:S(2)}, u32[]{:S(2)}) collective-permute-start(bf16[2048,384]{1,0:T(8,128)(2,1)S(1)} %pad_maximum_fusion.rest_5_.rest_6_.rest_7_), channel_id=1, source_target_pairs={{0,8},{1,9},{2,10},{3,11},{4,12},{5,13},{6,14},{7,15},{16,24},{17,... | collective-permute-start | bytes 4718600 | tf_op jit(solution)/shard_map/ppermute | solution.py:242
  36.7 0.7 fusion.4
  37.4 0.7 compare_and_fusion
  38.1 1.5 %convert_reduce_fusion.1 = s32[2048]{0:T(1024)S(1)} fusion(bf16[2048,640]{1,0:T(8,128)(2,1)} %copy-done.3), kind=kLoop, calls=%fused_computation.7 | loop fusion | flops 2048 | bytes 12288 | tf_op jit(solution)/shard_map/convert_element_type | solution.py:236
  39.7 0.0 copy-start.4
  39.7 0.6 gather_fusion
  40.3 0.1 select_bitcast_fusion.1
  40.4 0.7 slice.19.qdf_ref
  41.0 0.6 slice.20.qdl_ref
  41.6 1.4 %slice_reduce_fusion.1 = bf16[2048]{0:T(1024)(128)(2,1)S(1)} fusion(bf16[2048,640]{1,0:T(8,128)(2,1)} %copy-done.3), kind=kLoop, calls=%fused_computation.9 | loop fusion | bytes 8192 | tf_op jit(solution)/shard_map/slice | solution.py:236
  43.1 1.3 %copy.32 = s32[1,2048]{0,1:T(8,128)} copy(s32[1,2048]{1,0:T(1,128)S(1)} %bitcast.39) | data formatting | bytes 16384
  44.4 0.0 collective-permute-done.7.rest_0_.rest_1_.rest_2_
  44.4 0.0 copy-start.2
  44.4 0.4 slice_reduce_fusion
  44.9 0.7 convert_reduce_fusion.2
  45.6 1.1 %convert_reduce_fusion = s32[2048]{0:T(1024)} fusion(bf16[2048,384]{1,0:T(8,128)(2,1)S(1)} %collective-permute-done.7.rest_0_.rest_1_.rest_2_), kind=kLoop, calls=%fused_computation.6 | loop fusion | flops 2048 | bytes 12288 | tf_op jit(solution)/shard_map/convert_element_type | solution.py:244
  46.7 0.0 copy-done.1
  46.7 0.0 copy-done.4
  46.7 0.0 copy-done.2
  46.7 31.1 %shard_map.73 = bf16[2048,128]{1,0:T(8,128)(2,1)} custom-call(s32[1]{0:T(128)} %bitcast.1.qbase_ref, s32[4]{0:T(128)} %slice.19.qdf_ref, s32[4]{0:T(128)} %slice.20.qdl_ref, s32[8]{0:T(128)} %get-tuple-element.16.kminp_ref, s32[8]{0:T(128)} %get-tuple-element.17.kmaxp_ref, s32[8]{0:T(128)} %get-tuple-element.24.kmind_ref, s32[8]{0:T(128)} %get-tuple-element.23.kmaxd_ref, ...), custom_call_target="tpu_custom_call" | custom-call | tf_op jit(solution)/shard_map/pallas_call | solution.py:148
  (19 shorter events, 0.4 us)
Async XLA Ops:
  0.0 33.1 %copy-start = (bf16[512,128]{1,0:T(8,128)(2,1)S(1)}, bf16[512,128]{1,0:T(8,128)(2,1)}, u32[]{:S(2)}) copy-start(bf16[512,128]{1,0:T(8,128)(2,1)} %param.11) | copy-start | bytes 393220
  2.9 8.8 %collective-permute-start = (bf16[256,640]{1,0:T(8,128)(2,1)}, bf16[256,640]{1,0:T(8,128)(2,1)S(1)}, u32[]{:S(2)}, u32[]{:S(2)}) collective-permute-start(bf16[256,640]{1,0:T(8,128)(2,1)} %get-tuple-element.26), channel_id=1, source_target_pairs={{0,2},{2,4},{4,6},{6,7},{7,5},{5,3},{3,1},{1,0},{8,10},{10,12},{12... | collective-permute-start | bytes 983048 | tf_op jit(solution)/shard_map/ppermute | solution.py:187
  4.2 8.5 %collective-permute-start.1 = (bf16[256,640]{1,0:T(8,128)(2,1)}, bf16[256,640]{1,0:T(8,128)(2,1)S(1)}, u32[]{:S(2)}, u32[]{:S(2)}) collective-permute-start(bf16[256,640]{1,0:T(8,128)(2,1)} %get-tuple-element.26), channel_id=1, source_target_pairs={{2,0},{4,2},{6,4},{7,6},{5,7},{3,5},{1,3},{0,1},{10,8},{12,10},{14... | collective-permute-start | bytes 983048 | tf_op jit(solution)/shard_map/ppermute | solution.py:189
  12.7 7.3 %collective-permute-start.2 = (bf16[256,640]{1,0:T(8,128)(2,1)S(1)}, bf16[256,640]{1,0:T(8,128)(2,1)S(1)}, u32[]{:S(2)}, u32[]{:S(2)}) collective-permute-start(bf16[256,640]{1,0:T(8,128)(2,1)S(1)} %collective-permute-done), channel_id=1, source_target_pairs={{0,2},{2,4},{4,6},{6,7},{7,5},{5,3},{3,1},{1,0},{8,10},{10,12},{12... | collective-permute-start | bytes 983048 | tf_op jit(solution)/shard_map/ppermute | solution.py:187
  13.9 7.4 %collective-permute-start.3 = (bf16[256,640]{1,0:T(8,128)(2,1)S(1)}, bf16[256,640]{1,0:T(8,128)(2,1)S(1)}, u32[]{:S(2)}, u32[]{:S(2)}) collective-permute-start(bf16[256,640]{1,0:T(8,128)(2,1)S(1)} %collective-permute-done.1), channel_id=1, source_target_pairs={{2,0},{4,2},{6,4},{7,6},{5,7},{3,5},{1,3},{0,1},{10,8},{12,10},{14... | collective-permute-start | bytes 983048 | tf_op jit(solution)/shard_map/ppermute | solution.py:189
  20.0 6.4 %collective-permute-start.4 = (bf16[256,640]{1,0:T(8,128)(2,1)S(1)}, bf16[256,640]{1,0:T(8,128)(2,1)S(1)}, u32[]{:S(2)}, u32[]{:S(2)}) collective-permute-start(bf16[256,640]{1,0:T(8,128)(2,1)S(1)} %collective-permute-done.2), channel_id=1, source_target_pairs={{0,2},{2,4},{4,6},{6,7},{7,5},{5,3},{3,1},{1,0},{8,10},{10,12},{12... | collective-permute-start | bytes 983048 | tf_op jit(solution)/shard_map/ppermute | solution.py:187
  21.3 6.4 %collective-permute-start.5 = (bf16[256,640]{1,0:T(8,128)(2,1)S(1)}, bf16[256,640]{1,0:T(8,128)(2,1)S(1)}, u32[]{:S(2)}, u32[]{:S(2)}) collective-permute-start(bf16[256,640]{1,0:T(8,128)(2,1)S(1)} %collective-permute-done.3), channel_id=1, source_target_pairs={{2,0},{4,2},{6,4},{7,6},{5,7},{3,5},{1,3},{0,1},{10,8},{12,10},{14... | collective-permute-start | bytes 983048 | tf_op jit(solution)/shard_map/ppermute | solution.py:189
  26.4 6.5 %collective-permute-start.6 = (bf16[256,640]{1,0:T(8,128)(2,1)S(1)}, bf16[256,640]{1,0:T(8,128)(2,1)S(1)}, u32[]{:S(2)}, u32[]{:S(2)}) collective-permute-start(bf16[256,640]{1,0:T(8,128)(2,1)S(1)} %collective-permute-done.4), channel_id=1, source_target_pairs={{0,2},{2,4},{4,6},{6,7},{7,5},{5,3},{3,1},{1,0},{8,10},{10,12},{12... | collective-permute-start | bytes 983048 | tf_op jit(solution)/shard_map/ppermute | solution.py:187
  27.8 6.7 %copy-start.5 = (bf16[512,128]{1,0:T(8,128)(2,1)S(1)}, bf16[512,128]{1,0:T(8,128)(2,1)}, u32[]{:S(2)}) copy-start(bf16[512,128]{1,0:T(8,128)(2,1)} %param.10) | copy-start | bytes 393220
  33.0 1.5 %copy-start.3 = (bf16[2048,640]{1,0:T(8,128)(2,1)}, bf16[2048,640]{1,0:T(8,128)(2,1)S(1)}, u32[]{:S(2)}) copy-start(bf16[2048,640]{1,0:T(8,128)(2,1)S(1)} %constant_dynamic-update-slice_fusion) | copy-start | bytes 7864324
  35.4 11.2 %copy-start.1 = (bf16[2048,384]{1,0:T(8,128)(2,1)}, bf16[2048,384]{1,0:T(8,128)(2,1)S(1)}, u32[]{:S(2)}) copy-start(bf16[2048,384]{1,0:T(8,128)(2,1)S(1)} %pad_maximum_fusion.rest_5_.rest_6_.rest_7_) | copy-start | bytes 4718596
  35.4 9.0 %collective-permute-start.7 = (bf16[2048,384]{1,0:T(8,128)(2,1)S(1)}, bf16[2048,384]{1,0:T(8,128)(2,1)S(1)}, u32[]{:S(2)}, u32[]{:S(2)}) collective-permute-start(bf16[2048,384]{1,0:T(8,128)(2,1)S(1)} %pad_maximum_fusion.rest_5_.rest_6_.rest_7_), channel_id=1, source_target_pairs={{0,8},{1,9},{2,10},{3,11},{4,12},{5,13},{6,14},{7,15},{16,24},{17,... | collective-permute-start | bytes 4718600 | tf_op jit(solution)/shard_map/ppermute | solution.py:242
  39.7 7.0 %copy-start.4 = (s32[2048]{0:T(1024)}, s32[2048]{0:T(1024)S(1)}, u32[]{:S(2)}) copy-start(s32[2048]{0:T(1024)S(1)} %convert_reduce_fusion.1) | copy-start | bytes 24580
  44.4 2.2 %copy-start.2 = (bf16[2048,384]{1,0:T(8,128)(2,1)}, bf16[2048,384]{1,0:T(8,128)(2,1)S(1)}, u32[]{:S(2)}) copy-start(bf16[2048,384]{1,0:T(8,128)(2,1)S(1)} %collective-permute-done.7.rest_0_.rest_1_.rest_2_) | copy-start | bytes 4718596
where the time goes:
time: 77.4 us; the launch traced here: 77.7 us
  Pallas kernels  31.1 us (40%)
  waiting for transfers between devices  19 us (25%)
  local copies, waits for them, and re-layouts  11.1 us (14%)
  other arithmetic  8.01 us (10%)
  starting transfers between devices  6.95 us (9%)
  matrix products  1.41 us (2%)
    pallas_call x1, Pallas kernels, flash(): pl.pallas_call(kernel, grid_spec=grid_spec, out_shape=jax.ShapeDtypeStruc...  31.1 us
    ppermute x4, waiting for transfers between devices, ring_gather(): moving_f = lax.ppermute(moving_f, 'tp', forward)  18 us
    unnamed x29, local copies, waits for them, and re-layouts  7.08 us
    ppermute x4, starting transfers between devices, ring_gather(): moving_f = lax.ppermute(moving_f, 'tp', forward)  4.93 us
  transfers between devices with their start and end apart: 8, of which 5 were waited for; matrix products, arithmetic and copies ran while one was open for 17% of the time, Pallas kernels for 0%

commit v1 on v0

--- a/solution.py
+++ b/solution.py
@@ -62,8 +62,6 @@
             m_new = jnp.maximum(m_prev, jnp.max(scores, axis=1, keepdims=True))
             alpha = jnp.exp(m_prev - m_new)
             weights = jnp.exp(scores - m_new)
-            if masked:
-                weights = jnp.where(visible, weights, jnp.float32(0.0))
             l_sc[...] = alpha * l_sc[...] + jnp.sum(weights, axis=1, keepdims=True)
             acc_sc[...] = alpha * acc_sc[...] + jnp.dot(
                 weights.astype(jnp.bfloat16),
@@ -173,7 +171,7 @@
     return jnp.asarray(source_of)[me], jnp.asarray(slot_of)[me]
 
 
-def ring_gather(block, order, early):
+def ring_gather(block, order, early, source_of):
     count = len(order)
     place = {device: number for number, device in enumerate(order)}
     forward = [(order[i], order[(i + 1) % count]) for i in range(count)]
@@ -192,7 +190,11 @@
         arrived.append(moving_f)
         if step <= behind:
             arrived.append(moving_b)
-    return jnp.concatenate(arrived, axis=0), early
+    rows = block.shape[0]
+    placed = jnp.zeros((count * rows, block.shape[1]), block.dtype)
+    for number, piece in enumerate(arrived):
+        placed = lax.dynamic_update_slice(placed, piece, (source_of[number] * rows, 0))
+    return placed, early
 
 
 def body(queries, latent_rows, doc_ids, key_weight, value_weight, *, order):
@@ -210,9 +212,7 @@
     )
     chunk = jnp.concatenate([latent_rows, doc_column], axis=1)
     source_of, slot_of = ring_tables(order)
-    offsets = (
-        source_of[:, None] * chunk_rows + jnp.arange(chunk_rows, dtype=jnp.int32)[None, :]
-    ).reshape(block_rows)
+    offsets = jnp.arange(block_rows, dtype=jnp.int32)
     positions = []
     for distance in range(cycle_size - 1, 0, -1):
         source = cycle_index - distance
@@ -223,7 +223,7 @@
     query_base = (cycle_index * block_rows).astype(jnp.int32).reshape(1)
     query_heads = jnp.transpose(queries, (1, 0, 2))
     early = (tuple(pos.reshape(1, -1) for pos in positions), pos_tables, query_base, query_heads)
-    gathered, early = ring_gather(chunk, order, early)
+    gathered, early = ring_gather(chunk, order, early, source_of)
     positions, pos_tables, query_base, query_heads = early
     latent_part = gathered[:, :KV_RANK]
     key_heads = jnp.dot(latent_part, key_weight, preferred_element_type=jnp.float32).astype(
@@ -234,7 +234,7 @@
     )
     pack = jnp.concatenate([key_heads, value_heads, gathered[:, KV_RANK:]], axis=1)
     docs = gathered[:, width].astype(jnp.int32)
-    query_docs = jnp.take(docs.reshape(chunks, chunk_rows), slot_of, axis=0).reshape(block_rows)
+    query_docs = docs
 
     packs, docs_rows = [], []
     for distance in range(cycle_size - 1, 0, -1):

time: 77.4 us -> 71.7 us (0.926)
  the two profiles are of different devices: /device:TPU:17 before, /device:TPU:0 now
where the time goes in v1:
time: 71.7 us
  Pallas kernels  19.3 us (27%)
  waiting for transfers between devices  16.9 us (24%)
  starting transfers between devices  10.1 us (14%)
  local copies, waits for them, and re-layouts  9.9 us (14%)
  other arithmetic  8.79 us (12%)
  between operations  5.25 us (7%)
  matrix products  1.41 us (2%)
    pallas_call x1, Pallas kernels, flash(): pl.pallas_call(kernel, grid_spec=grid_spec, out_shape=jax.ShapeDtypeStruc...  19.3 us
    ppermute x4, waiting for transfers between devices, ring_gather(): moving_f = lax.ppermute(moving_f, 'tp', forward)  15.4 us
    ppermute x4, starting transfers between devices, ring_gather(): moving_f = lax.ppermute(moving_f, 'tp', forward)  7.75 us
    unnamed x14, local copies, waits for them, and re-layouts  4.15 us
    convert_element_type x2, other arithmetic, body(): docs = gathered[:, width].astype(jnp.int32)  3.88 us
    dynamic_update_slice x7, local copies, waits for them, and re-layouts, ring_gather(): lax.dynamic_update_slice(placed, piece, (source_of[number] * rows, 0))  2.24 us
    ppermute x3, waiting for transfers between devices, ring_gather(): moving_b = lax.ppermute(moving_b, 'tp', backward)  1.55 us
  transfers between devices with their start and end apart: 8, of which 5 were waited for; matrix products, arithmetic and copies ran while one was open for 15% of the time, Pallas kernels for 0%

profile of v1, /device:TPU:0, one launch (start us, length us, event | category | flops | bytes accessed | tf_op | source)
XLA Modules:
  0.0 71.7 jit_solution(16889570600902744849)
XLA Ops:
  0.0 0.0 copy-start
  0.0 0.7 %constant_dynamic-slice_fusion = s32[1,8]{1,0:T(1,128)S(1)} fusion(s32[8,8]{1,0:T(8,128)} %constant.42.clone, s32[]{:T(128)S(6)} %select_n.51), kind=kLoop, calls=%fused_computation.30 | loop fusion | bytes 68 | tf_op jit(solution)/shard_map/dynamic_slice | solution.py:171
  0.7 0.7 fusion.6
  2.1 0.7 convert_element_type.51
  2.7 0.1 broadcast_in_dim.20
  2.9 1.2 %copy.16 = bf16[256,576]{1,0:T(8,128)(2,1)S(1)} copy(bf16[256,576]{0,1:T(8,128)(2,1)} %param.7) | data formatting | bytes 589824 | tf_op args[1]
  4.0 0.1 pad.9.clone
  4.1 0.2 broadcast_in_dim.19
  4.3 0.8 %constant_dynamic-update-slice_fusion.7 = (bf16[2048,640]{1,0:T(8,128)(2,1)S(1)}, bf16[256,640]{1,0:T(8,128)(2,1)}) fusion(bf16[2048,640]{1,0:T(8,128)(2,1)S(1)} %broadcast_in_dim.19, s32[]{:T(128)S(6)} %select_n.52, bf16[640]{0:T(1024)(128)(2,1)S(1)} %pad.9.clone, bf16[256,1]{1,0:T(8,128)(2,1)S(1)} %broadcast_in_dim.20, bf16[256,576]{1,0:T(8,128)(2,1)S(1)} %copy.16), kind=kLoop, calls=%fused_computation.29 | loop fusion | flops 983040 | bytes 1050628 | tf_op jit(solution)/shard_map/dynamic_update_slice | solution.py:196
  5.2 3.0 %collective-permute-start = (bf16[256,640]{1,0:T(8,128)(2,1)}, bf16[256,640]{1,0:T(8,128)(2,1)S(1)}, u32[]{:S(2)}, u32[]{:S(2)}) collective-permute-start(bf16[256,640]{1,0:T(8,128)(2,1)} %get-tuple-element.26), channel_id=1, source_target_pairs={{0,2},{2,4},{4,6},{6,7},{7,5},{5,3},{3,1},{1,0},{8,10},{10,12},{12... | collective-permute-start | bytes 983048 | tf_op jit(solution)/shard_map/ppermute | solution.py:185
  8.2 0.0 collective-permute-start.1
  8.2 2.2 %copy.18 = bf16[2048,1,192]{2,0,1:T(8,128)(2,1)} copy(bf16[2048,1,192]{0,2,1:T(8,128)(2,1)} %param.6) | data formatting | bytes 1572864 | tf_op args[0]
  10.4 0.7 %fusion.3 = (s32[8]{0:T(128)}, s32[8]{0:T(128)}) fusion(s32[4,512]{1,0:T(4,128)S(1)} %get-tuple-element.38, s32[4,512]{1,0:T(4,128)S(1)} %get-tuple-element.37), kind=kLoop, calls=%fused_computation.15 | loop fusion | flops 12272 | bytes 16448 | tf_op jit(solution)/shard_map/reduce_max | solution.py:222
  11.2 0.6 broadcast_select_fusion
  11.8 4.2 %collective-permute-done = bf16[256,640]{1,0:T(8,128)(2,1)S(1)} collective-permute-done((bf16[256,640]{1,0:T(8,128)(2,1)}, bf16[256,640]{1,0:T(8,128)(2,1)S(1)}, u32[]{:S(2)}, u32[]{:S(2)}) %collective-permute-start) | collective-permute-done | bytes 327712 | tf_op jit(solution)/shard_map/ppermute | solution.py:185
  16.0 1.5 %collective-permute-done.1 = bf16[256,640]{1,0:T(8,128)(2,1)S(1)} collective-permute-done((bf16[256,640]{1,0:T(8,128)(2,1)}, bf16[256,640]{1,0:T(8,128)(2,1)S(1)}, u32[]{:S(2)}, u32[]{:S(2)}) %collective-permute-start.1) | collective-permute-done | bytes 327712 | tf_op jit(solution)/shard_map/ppermute | solution.py:187
  17.6 1.6 %collective-permute-start.2 = (bf16[256,640]{1,0:T(8,128)(2,1)S(1)}, bf16[256,640]{1,0:T(8,128)(2,1)}, u32[]{:S(2)}, u32[]{:S(2)}) collective-permute-start(bf16[256,640]{1,0:T(8,128)(2,1)S(1)} %collective-permute-done), channel_id=1, source_target_pairs={{0,2},{2,4},{4,6},{6,7},{7,5},{5,3},{3,1},{1,0},{8,10},{10,12},{12... | collective-permute-start | bytes 983048 | tf_op jit(solution)/shard_map/ppermute | solution.py:185
  19.1 0.4 collective-permute-start.3
  24.0 1.9 %collective-permute-done.2 = bf16[256,640]{1,0:T(8,128)(2,1)} collective-permute-done((bf16[256,640]{1,0:T(8,128)(2,1)S(1)}, bf16[256,640]{1,0:T(8,128)(2,1)}, u32[]{:S(2)}, u32[]{:S(2)}) %collective-permute-start.2) | collective-permute-done | bytes 327712 | tf_op jit(solution)/shard_map/ppermute | solution.py:185
  25.9 1.6 %collective-permute-start.4 = (bf16[256,640]{1,0:T(8,128)(2,1)}, bf16[256,640]{1,0:T(8,128)(2,1)S(1)}, u32[]{:S(2)}, u32[]{:S(2)}) collective-permute-start(bf16[256,640]{1,0:T(8,128)(2,1)} %collective-permute-done.2), channel_id=1, source_target_pairs={{0,2},{2,4},{4,6},{6,7},{7,5},{5,3},{3,1},{1,0},{8,10},{10,12},{12... | collective-permute-start | bytes 983048 | tf_op jit(solution)/shard_map/ppermute | solution.py:185
  27.6 0.0 collective-permute-done.3
  27.6 0.5 collective-permute-start.5
  28.1 1.0 %constant_dynamic-update-slice_fusion.4 = bf16[2048,640]{1,0:T(8,128)(2,1)S(1)} fusion(bf16[2048,640]{1,0:T(8,128)(2,1)S(1)} %constant_dynamic-update-slice_fusion.5, bf16[256,640]{1,0:T(8,128)(2,1)} %collective-permute-done.2, s32[]{:T(128)S(6)} %select_n.55), kind=kLoop, calls=%fused_computation.26 | loop fusion | bytes 655364 | tf_op jit(solution)/shard_map/dynamic_update_slice | solution.py:196
  29.1 4.9 %collective-permute-done.4 = bf16[256,640]{1,0:T(8,128)(2,1)S(1)} collective-permute-done((bf16[256,640]{1,0:T(8,128)(2,1)}, bf16[256,640]{1,0:T(8,128)(2,1)S(1)}, u32[]{:S(2)}, u32[]{:S(2)}) %collective-permute-start.4) | collective-permute-done | bytes 327712 | tf_op jit(solution)/shard_map/ppermute | solution.py:185
  34.0 1.6 %collective-permute-start.6 = (bf16[256,640]{1,0:T(8,128)(2,1)S(1)}, bf16[256,640]{1,0:T(8,128)(2,1)S(1)}, u32[]{:S(2)}, u32[]{:S(2)}) collective-permute-start(bf16[256,640]{1,0:T(8,128)(2,1)S(1)} %collective-permute-done.4), channel_id=1, source_target_pairs={{0,2},{2,4},{4,6},{6,7},{7,5},{5,3},{3,1},{1,0},{8,10},{10,12},{12... | collective-permute-start | bytes 983048 | tf_op jit(solution)/shard_map/ppermute | solution.py:185
  35.6 1.0 %constant_dynamic-update-slice_fusion.3 = bf16[2048,640]{1,0:T(8,128)(2,1)S(1)} fusion(bf16[2048,640]{1,0:T(8,128)(2,1)S(1)} %constant_dynamic-update-slice_fusion.4, bf16[256,640]{1,0:T(8,128)(2,1)} %collective-permute-done.3, s32[]{:T(128)S(6)} %select_n.56), kind=kLoop, calls=%fused_computation.25 | loop fusion | bytes 655364 | tf_op jit(solution)/shard_map/dynamic_update_slice | solution.py:196
  36.7 0.0 collective-permute-done.5
  36.7 0.0 copy-start.5
  36.7 4.4 %collective-permute-done.6 = bf16[256,640]{1,0:T(8,128)(2,1)S(1)} collective-permute-done((bf16[256,640]{1,0:T(8,128)(2,1)S(1)}, bf16[256,640]{1,0:T(8,128)(2,1)S(1)}, u32[]{:S(2)}, u32[]{:S(2)}) %collective-permute-start.6) | collective-permute-done | bytes 327712 | tf_op jit(solution)/shard_map/ppermute | solution.py:185
  41.1 0.0 copy-start.3
  41.2 0.0 copy-done
  41.2 0.7 convolution_convert_fusion
  41.9 0.7 %copy-done.3 = bf16[2048,640]{1,0:T(8,128)(2,1)} copy-done((bf16[2048,640]{1,0:T(8,128)(2,1)}, bf16[2048,640]{1,0:T(8,128)(2,1)S(1)}, u32[]{:S(2)}) %copy-start.3) | copy-done | bytes 2621464
  42.6 0.0 copy-done.5
  42.6 0.7 convolution_convert_fusion.1
  43.4 0.2 pad_maximum_fusion.rest_5_.rest_6_.rest_7_
  43.6 0.0 copy-start.1
  43.6 1.4 %collective-permute-start.7 = (bf16[2048,384]{1,0:T(8,128)(2,1)S(1)}, bf16[2048,384]{1,0:T(8,128)(2,1)S(1)}, u32[]{:S(2)}, u32[]{:S(2)}) collective-permute-start(bf16[2048,384]{1,0:T(8,128)(2,1)S(1)} %pad_maximum_fusion.rest_5_.rest_6_.rest_7_), channel_id=1, source_target_pairs={{0,8},{1,9},{2,10},{3,11},{4,12},{5,13},{6,14},{7,15},{16,24},{17,... | collective-permute-start | bytes 4718600 | tf_op jit(solution)/shard_map/ppermute | solution.py:242
  45.0 1.5 %fusion.2 = s32[2048]{0:T(1024)S(1)} fusion(bf16[2048,640]{1,0:T(8,128)(2,1)} %copy-done.3), kind=kLoop, calls=%fused_computation.10 | loop fusion | flops 2048 | bytes 12288 | tf_op jit(solution)/shard_map/convert_element_type | solution.py:236
  46.5 0.0 copy-start.4
  46.5 0.7 slice.59.qdf_ref
  47.2 0.6 slice.60.qdl_ref
  47.8 2.3 %slice_convert_fusion = (s32[2048,1]{1,0:T(8,128)}, bf16[2048]{0:T(1024)(128)(2,1)S(1)}) fusion(bf16[2048,640]{1,0:T(8,128)(2,1)} %copy-done.3), kind=kLoop, calls=%fused_computation.8 | loop fusion | flops 2048 | bytes 16384 | tf_op jit(solution)/shard_map/convert_element_type | solution.py:236
  50.2 0.0 collective-permute-done.7.rest_0_.rest_1_.rest_2_
  50.2 0.0 copy-start.2
  50.2 0.4 slice_reduce_fusion
  50.6 0.7 convert_reduce_fusion.1
  51.3 1.1 %convert_reduce_fusion = s32[2048]{0:T(1024)} fusion(bf16[2048,384]{1,0:T(8,128)(2,1)S(1)} %collective-permute-done.7.rest_0_.rest_1_.rest_2_), kind=kLoop, calls=%fused_computation.5 | loop fusion | flops 2048 | bytes 12288 | tf_op jit(solution)/shard_map/convert_element_type | solution.py:244
  52.4 0.0 copy-done.1
  52.4 0.0 copy-done.4
  52.4 0.0 copy-done.2
  52.4 19.3 %shard_map.64 = bf16[2048,128]{1,0:T(8,128)(2,1)} custom-call(s32[1]{0:T(128)} %bitcast.qbase_ref, s32[4]{0:T(128)} %slice.59.qdf_ref, s32[4]{0:T(128)} %slice.60.qdl_ref, s32[8]{0:T(128)} %get-tuple-element.16.kminp_ref, s32[8]{0:T(128)} %get-tuple-element.17.kmaxp_ref, s32[8]{0:T(128)} %get-tuple-element.24.kmind_ref, s32[8]{0:T(128)} %get-tuple-element.23.kmaxd_ref, ...), custom_call_target="tpu_custom_call" | custom-call | tf_op jit(solution)/shard_map/pallas_call | solution.py:146
  (10 shorter events, 0.3 us)
Async XLA Ops:
  0.0 41.2 %copy-start = (bf16[512,128]{1,0:T(8,128)(2,1)S(1)}, bf16[512,128]{1,0:T(8,128)(2,1)}, u32[]{:S(2)}) copy-start(bf16[512,128]{1,0:T(8,128)(2,1)} %param.10) | copy-start | bytes 393220
  5.2 10.9 %collective-permute-start = (bf16[256,640]{1,0:T(8,128)(2,1)}, bf16[256,640]{1,0:T(8,128)(2,1)S(1)}, u32[]{:S(2)}, u32[]{:S(2)}) collective-permute-start(bf16[256,640]{1,0:T(8,128)(2,1)} %get-tuple-element.26), channel_id=1, source_target_pairs={{0,2},{2,4},{4,6},{6,7},{7,5},{5,3},{3,1},{1,0},{8,10},{10,12},{12... | collective-permute-start | bytes 983048 | tf_op jit(solution)/shard_map/ppermute | solution.py:185
  8.2 9.4 %collective-permute-start.1 = (bf16[256,640]{1,0:T(8,128)(2,1)}, bf16[256,640]{1,0:T(8,128)(2,1)S(1)}, u32[]{:S(2)}, u32[]{:S(2)}) collective-permute-start(bf16[256,640]{1,0:T(8,128)(2,1)} %get-tuple-element.26), channel_id=1, source_target_pairs={{2,0},{4,2},{6,4},{7,6},{5,7},{3,5},{1,3},{0,1},{10,8},{12,10},{14... | collective-permute-start | bytes 983048 | tf_op jit(solution)/shard_map/ppermute | solution.py:187
  17.6 8.4 %collective-permute-start.2 = (bf16[256,640]{1,0:T(8,128)(2,1)S(1)}, bf16[256,640]{1,0:T(8,128)(2,1)}, u32[]{:S(2)}, u32[]{:S(2)}) collective-permute-start(bf16[256,640]{1,0:T(8,128)(2,1)S(1)} %collective-permute-done), channel_id=1, source_target_pairs={{0,2},{2,4},{4,6},{6,7},{7,5},{5,3},{3,1},{1,0},{8,10},{10,12},{12... | collective-permute-start | bytes 983048 | tf_op jit(solution)/shard_map/ppermute | solution.py:185
  19.1 8.5 %collective-permute-start.3 = (bf16[256,640]{1,0:T(8,128)(2,1)S(1)}, bf16[256,640]{1,0:T(8,128)(2,1)}, u32[]{:S(2)}, u32[]{:S(2)}) collective-permute-start(bf16[256,640]{1,0:T(8,128)(2,1)S(1)} %collective-permute-done.1), channel_id=1, source_target_pairs={{2,0},{4,2},{6,4},{7,6},{5,7},{3,5},{1,3},{0,1},{10,8},{12,10},{14... | collective-permute-start | bytes 983048 | tf_op jit(solution)/shard_map/ppermute | solution.py:187
  25.9 8.1 %collective-permute-start.4 = (bf16[256,640]{1,0:T(8,128)(2,1)}, bf16[256,640]{1,0:T(8,128)(2,1)S(1)}, u32[]{:S(2)}, u32[]{:S(2)}) collective-permute-start(bf16[256,640]{1,0:T(8,128)(2,1)} %collective-permute-done.2), channel_id=1, source_target_pairs={{0,2},{2,4},{4,6},{6,7},{7,5},{5,3},{3,1},{1,0},{8,10},{10,12},{12... | collective-permute-start | bytes 983048 | tf_op jit(solution)/shard_map/ppermute | solution.py:185
  27.6 9.1 %collective-permute-start.5 = (bf16[256,640]{1,0:T(8,128)(2,1)}, bf16[256,640]{1,0:T(8,128)(2,1)S(1)}, u32[]{:S(2)}, u32[]{:S(2)}) collective-permute-start(bf16[256,640]{1,0:T(8,128)(2,1)} %collective-permute-done.3), channel_id=1, source_target_pairs={{2,0},{4,2},{6,4},{7,6},{5,7},{3,5},{1,3},{0,1},{10,8},{12,10},{14... | collective-permute-start | bytes 983048 | tf_op jit(solution)/shard_map/ppermute | solution.py:187
  34.0 7.1 %collective-permute-start.6 = (bf16[256,640]{1,0:T(8,128)(2,1)S(1)}, bf16[256,640]{1,0:T(8,128)(2,1)S(1)}, u32[]{:S(2)}, u32[]{:S(2)}) collective-permute-start(bf16[256,640]{1,0:T(8,128)(2,1)S(1)} %collective-permute-done.4), channel_id=1, source_target_pairs={{0,2},{2,4},{4,6},{6,7},{7,5},{5,3},{3,1},{1,0},{8,10},{10,12},{12... | collective-permute-start | bytes 983048 | tf_op jit(solution)/shard_map/ppermute | solution.py:185
  36.7 5.9 %copy-start.5 = (bf16[512,128]{1,0:T(8,128)(2,1)S(1)}, bf16[512,128]{1,0:T(8,128)(2,1)}, u32[]{:S(2)}) copy-start(bf16[512,128]{1,0:T(8,128)(2,1)} %param.9) | copy-start | bytes 393220
  41.1 1.5 %copy-start.3 = (bf16[2048,640]{1,0:T(8,128)(2,1)}, bf16[2048,640]{1,0:T(8,128)(2,1)S(1)}, u32[]{:S(2)}) copy-start(bf16[2048,640]{1,0:T(8,128)(2,1)S(1)} %constant_dynamic-update-slice_fusion) | copy-start | bytes 7864324
  43.6 8.8 %copy-start.1 = (bf16[2048,384]{1,0:T(8,128)(2,1)}, bf16[2048,384]{1,0:T(8,128)(2,1)S(1)}, u32[]{:S(2)}) copy-start(bf16[2048,384]{1,0:T(8,128)(2,1)S(1)} %pad_maximum_fusion.rest_5_.rest_6_.rest_7_) | copy-start | bytes 4718596
  43.6 6.6 %collective-permute-start.7 = (bf16[2048,384]{1,0:T(8,128)(2,1)S(1)}, bf16[2048,384]{1,0:T(8,128)(2,1)S(1)}, u32[]{:S(2)}, u32[]{:S(2)}) collective-permute-start(bf16[2048,384]{1,0:T(8,128)(2,1)S(1)} %pad_maximum_fusion.rest_5_.rest_6_.rest_7_), channel_id=1, source_target_pairs={{0,8},{1,9},{2,10},{3,11},{4,12},{5,13},{6,14},{7,15},{16,24},{17,... | collective-permute-start | bytes 4718600 | tf_op jit(solution)/shard_map/ppermute | solution.py:242
  46.5 5.9 %copy-start.4 = (s32[2048]{0:T(1024)}, s32[2048]{0:T(1024)S(1)}, u32[]{:S(2)}) copy-start(s32[2048]{0:T(1024)S(1)} %fusion.2) | copy-start | bytes 24580
  50.2 2.2 %copy-start.2 = (bf16[2048,384]{1,0:T(8,128)(2,1)}, bf16[2048,384]{1,0:T(8,128)(2,1)S(1)}, u32[]{:S(2)}) copy-start(bf16[2048,384]{1,0:T(8,128)(2,1)S(1)} %collective-permute-done.7.rest_0_.rest_1_.rest_2_) | copy-start | bytes 4718596
